TPU v7x, 256 devices: a whole 4x4x8 slice. The times are simulated.
256 devices in a mesh: dp: 2 (over y_hi), ctx: 64 (over y_lo, x, z), head: 2 (over core).
Axes of the slice: x: 4, y: 4 (y_hi: 2, y_lo: 2; y = y_hi * 2 + y_lo), z: 8, core: 2. Of those that a mesh axis runs over, the one named last changes fastest.
Arguments:
- hidden_in: bfloat16 [2, 8192, 4096], P('dp', 'ctx'), may hold values from -16 to 16
- proj_weight: bfloat16 [4096, 2, 256], P(('dp', 'ctx'), None, 'head'), may hold values from -0.0029296875 to 0.0029296875
- values_in: bfloat16 [2, 8192, 4096], P('dp', 'ctx', 'head'), may hold values from -6 to 6
- gate_in: bfloat16 [2, 8192, 4096], P('dp', 'ctx', 'head'), may hold values from -6 to 6
- log_decay: float32 [2, 64, 8192], P('dp', 'head', 'ctx'), may hold values from -1 to 0, as said below
- skip_gain: float32 [64], P('head'), may hold values from 0.5 to 2
- grad_out: bfloat16 [2, 8192, 4096], P('dp', 'ctx', 'head'), may hold values from -6 to 6
Outputs:
- grad_input: bfloat16 [2, 8192, 4096], P('dp', 'ctx', 'head')
- grad_values: bfloat16 [2, 8192, 4096], P('dp', 'ctx', 'head')
- grad_gate: bfloat16 [2, 8192, 4096], P('dp', 'ctx', 'head')
- grad_proj: float32 [4096, 2, 256], P(('dp', 'ctx'), None, 'head')
Inputs may be any that keep to these rules, and one draw needn't show every extreme that they name: `log_decay`: logarithms of the per-token decay of each head's state; all values are at most zero.
All inputs are finite; a program needn't handle non-finite values.
Results may differ from a plain program's by a relative error of at most 0.011.
Values may be sent and summed in bfloat16 or wider, within the bound.
No kernel may reach another device: no remote copies, remote signals or barrier semaphores. Data moves between devices by JAX's collectives and lax.ppermute only.
A program may use at most 192 MiB of HBM per device.

v0:
```python
import jax
import jax.numpy as jnp
from jax import lax
from jax.sharding import PartitionSpec as P

HEAD_DIM = 64
STATE = 64
SPAN = 128


def carried_in(part, axis, combine, identity, reverse):
    count = lax.axis_size(axis)
    place = lax.axis_index(axis)
    ahead = count - 1 - place if reverse else place
    gathered = jax.tree.map(lambda a: lax.all_gather(a, axis), part)
    state = jax.tree.map(lambda a, e: jnp.zeros_like(a) + jnp.asarray(e, a.dtype), part, identity)

    def one(lap, state):
        source = count - 1 - lap if reverse else lap
        return combine(
            state, jax.tree.map(lambda a: lax.dynamic_index_in_dim(a, source, 0, False), gathered)
        )

    return lax.fori_loop(0, ahead, one, state)


def span_summary(b_vals, c_vals, x_vals, dy_round, rate_vals):
    block_len = x_vals.shape[0]
    head_count = x_vals.shape[1]
    group_count = b_vals.shape[1]
    per_group = head_count // group_count
    cumlog = jnp.cumsum(rate_vals, axis=1)
    final_log = cumlog[:, -1]
    to_end = jnp.exp(final_log[:, None] - cumlog)
    from_start = jnp.exp(cumlog)
    b_wide = b_vals.astype(jnp.float32)
    c_wide = c_vals.astype(jnp.float32)
    x_scaled = (x_vals.astype(jnp.float32) * to_end.T[:, :, None]).reshape(
        block_len, group_count, per_group, HEAD_DIM
    )
    dy_scaled = (dy_round.astype(jnp.float32) * from_start.T[:, :, None]).reshape(
        block_len, group_count, per_group, HEAD_DIM
    )
    state_part = jnp.einsum("qgn,qgkp->ngkp", b_wide, x_scaled, precision=lax.Precision.HIGHEST)
    adjoint_part = jnp.einsum("qgn,qgkp->ngkp", c_wide, dy_scaled, precision=lax.Precision.HIGHEST)
    return (jnp.exp(final_log), state_part.reshape(STATE, -1), adjoint_part.reshape(STATE, -1))


def span_full(
    b_vals,
    c_vals,
    x_vals,
    dy_round,
    rate_vals,
    skip_vals,
    state_in,
    adjoint_out,
    dout_vals,
    gate_vals,
):
    block_len = x_vals.shape[0]
    head_count = x_vals.shape[1]
    group_count = b_vals.shape[1]
    per_group = head_count // group_count
    cumlog = jnp.cumsum(rate_vals, axis=1)
    final_log = cumlog[:, -1]
    to_end = jnp.exp(final_log[:, None] - cumlog)
    from_start = jnp.exp(cumlog)
    causal = jnp.arange(block_len)[:, None] >= jnp.arange(block_len)[None, :]
    log_gaps = cumlog[:, :, None] - cumlog[:, None, :]
    decays = jnp.where(causal[None], jnp.exp(jnp.where(causal[None], log_gaps, 0.0)), 0.0)
    b_wide = b_vals.astype(jnp.float32)
    c_wide = c_vals.astype(jnp.float32)
    cb_dots = jnp.einsum("tgn,sgn->gts", c_vals, b_vals, preferred_element_type=jnp.float32)
    mixer_bf = (decays * jnp.repeat(cb_dots, per_group, axis=0)).astype(jnp.bfloat16)
    state_four = state_in.reshape(STATE, group_count, per_group, HEAD_DIM)
    adjoint_four = adjoint_out.reshape(STATE, group_count, per_group, HEAD_DIM)
    y_intra = jnp.einsum("hts,shp->thp", mixer_bf, x_vals, preferred_element_type=jnp.float32)
    y_inter = jnp.einsum(
        "tgn,ngkp->tgkp", c_wide, state_four, precision=lax.Precision.HIGHEST
    ).reshape(block_len, head_count, HEAD_DIM)
    x_wide = x_vals.astype(jnp.float32)
    output_pre = y_intra + y_inter * from_start.T[:, :, None] + skip_vals[None, :, None] * x_wide
    gate_wide = gate_vals.astype(jnp.float32)
    gate_sig = jax.nn.sigmoid(gate_wide)
    grad_gate = (
        dout_vals.astype(jnp.float32) * output_pre * gate_sig * (1.0 + gate_wide * (1.0 - gate_sig))
    ).astype(jnp.bfloat16)
    dy_wide = dy_round.astype(jnp.float32)
    x_inter = jnp.einsum(
        "sgn,ngkp->sgkp", b_wide, adjoint_four, precision=lax.Precision.HIGHEST
    ).reshape(block_len, head_count, HEAD_DIM)
    grad_vals = (
        jnp.einsum("hts,thp->shp", mixer_bf, dy_round, preferred_element_type=jnp.float32)
        + x_inter * to_end.T[:, :, None]
        + skip_vals[None, :, None] * dy_wide
    )
    mix_grad = (
        jnp.einsum("thp,shp->hts", dy_round, x_vals, preferred_element_type=jnp.float32) * decays
    )
    dots_grad = (
        mix_grad.reshape(group_count, per_group, block_len, block_len)
        .sum(axis=1)
        .astype(jnp.bfloat16)
    )
    dy_scaled = (dy_wide * from_start.T[:, :, None]).reshape(
        block_len, group_count, per_group, HEAD_DIM
    )
    x_scaled = (x_wide * to_end.T[:, :, None]).reshape(block_len, group_count, per_group, HEAD_DIM)
    c_grad = jnp.einsum(
        "gts,sgn->tgn", dots_grad, b_vals, preferred_element_type=jnp.float32
    ) + jnp.einsum("tgkp,ngkp->tgn", dy_scaled, state_four, precision=lax.Precision.HIGHEST)
    b_grad = jnp.einsum(
        "gts,tgn->sgn", dots_grad, c_vals, preferred_element_type=jnp.float32
    ) + jnp.einsum("sgkp,ngkp->sgn", x_scaled, adjoint_four, precision=lax.Precision.HIGHEST)
    return (grad_vals.astype(jnp.bfloat16), grad_gate, jnp.stack([b_grad, c_grad], axis=1))


def chain(earlier, later):
    return (earlier[0] * later[0], earlier[1] * jnp.repeat(later[0], HEAD_DIM)[None, :] + later[1])


def body(hidden_in, proj_weight, values_in, gate_in, log_decay, skip_gain, grad_out):
    tokens = hidden_in[0]
    tok_rows = tokens.shape[0]
    weight_local = proj_weight.reshape(proj_weight.shape[0], -1)
    col_count = weight_local.shape[1]
    weight_full = lax.all_gather(weight_local, ("dp", "ctx"), axis=0, tiled=True)
    bc_sums = jnp.dot(tokens, weight_full, preferred_element_type=jnp.float32)
    group_count = col_count // (2 * STATE)
    head_count = values_in.shape[2] // HEAD_DIM
    nblocks = tok_rows // SPAN
    bc_vals = bc_sums.astype(jnp.bfloat16).reshape(nblocks, SPAN, 2, group_count, STATE)
    x_vals = values_in[0].reshape(nblocks, SPAN, head_count, HEAD_DIM)
    gate_vals = gate_in[0].reshape(nblocks, SPAN, head_count, HEAD_DIM)
    dout_vals = grad_out[0].reshape(nblocks, SPAN, head_count, HEAD_DIM)
    dy_round = (dout_vals.astype(jnp.float32) * jax.nn.silu(gate_vals.astype(jnp.float32))).astype(
        jnp.bfloat16
    )
    rate_vals = log_decay[0].reshape(head_count, nblocks, SPAN)
    summaries = [
        span_summary(bc_vals[0, :, 0], bc_vals[0, :, 1], x_vals[0], dy_round[0], rate_vals[:, 0])
    ]
    dev_decay = jnp.ones((head_count,), jnp.float32)
    dev_state = jnp.zeros((STATE, head_count * HEAD_DIM), jnp.float32)
    dev_adjoint = jnp.zeros((STATE, head_count * HEAD_DIM), jnp.float32)
    block_id = 0
    dev_state = (
        dev_state * jnp.repeat(summaries[block_id][0], HEAD_DIM)[None, :] + summaries[block_id][1]
    )
    dev_decay = dev_decay * summaries[block_id][0]
    for block_id in reversed(range(nblocks)):
        dev_adjoint = (
            dev_adjoint * jnp.repeat(summaries[block_id][0], HEAD_DIM)[None, :]
            + summaries[block_id][2]
        )
    identity = (
        jnp.ones((head_count,), jnp.float32),
        jnp.zeros((STATE, head_count * HEAD_DIM), jnp.float32),
    )
    state_start = carried_in((dev_decay, dev_state), "ctx", chain, identity, False)[1]
    adjoint_end = carried_in((dev_decay, dev_adjoint), "ctx", chain, identity, True)[1]
    running = state_start
    block_id = 0
    states_in = running
    adjoints_out = [None] * nblocks
    running = adjoint_end
    for block_id in reversed(range(nblocks)):
        adjoints_out[block_id] = running
        running = (
            running * jnp.repeat(summaries[block_id][0], HEAD_DIM)[None, :] + summaries[block_id][2]
        )
    results = [
        span_full(
            bc_vals[0, :, 0],
            bc_vals[0, :, 1],
            x_vals[0],
            dy_round[0],
            rate_vals[:, 0],
            skip_gain,
            states_in,
            adjoints_out[0],
            dout_vals[0],
            gate_vals[0],
        )
    ]
    grad_values = jnp.concatenate([entry[0] for entry in results], axis=0).reshape(
        1, tok_rows, head_count * HEAD_DIM
    )
    grad_gate = jnp.concatenate([entry[1] for entry in results], axis=0).reshape(
        1, tok_rows, head_count * HEAD_DIM
    )
    grad_flat = (
        jnp.concatenate([entry[2] for entry in results], axis=0)
        .reshape(tok_rows, col_count)
        .astype(jnp.bfloat16)
    )
    input_terms = jnp.einsum(
        "tc,dc->td", grad_flat, weight_full, preferred_element_type=jnp.float32
    )
    grad_input = lax.psum_scatter(
        input_terms.astype(jnp.bfloat16), "head", scatter_dimension=1, tiled=True
    )[None]
    scale = 1.0 / (lax.axis_size("dp") * lax.axis_size("ctx") * tok_rows)
    grad_proj = lax.psum_scatter(
        jnp.einsum("td,tc->dc", tokens, grad_flat, preferred_element_type=jnp.float32) * scale,
        ("dp", "ctx"),
        scatter_dimension=0,
        tiled=True,
    )
    grad_proj = grad_proj.reshape(-1, 2, col_count // 2)
    return (grad_input, grad_values, grad_gate, grad_proj)


def solution(mesh):
    return jax.shard_map(
        body,
        mesh=mesh,
        in_specs=(
            P("dp", "ctx", None),
            P(("dp", "ctx"), None, "head"),
            P("dp", "ctx", "head"),
            P("dp", "ctx", "head"),
            P("dp", "head", "ctx"),
            P("head"),
            P("dp", "ctx", "head"),
        ),
        out_specs=(
            P("dp", "ctx", "head"),
            P("dp", "ctx", "head"),
            P("dp", "ctx", "head"),
            P(("dp", "ctx"), None, "head"),
        ),
        check_vma=False,
    )
```

profile of v0, /device:TPU:1, one launch (start us, length us, event | category | flops | bytes accessed | tf_op | source)
XLA Modules:
  0.0 1724.1 jit_solution(12229518481348502227)
XLA Ops:
  7.2 1.4 copy.67
  8.8 1.3 copy.44
  12.9 2.0 copy.46
  16.2 109.6 %all-gather.5.cloned.1.call-done = bf16[4096,256]{1,0:T(8,128)(2,1)} async-done(((bf16[32,256]{1,0:T(8,128)(2,1)}), bf16[4096,256]{1,0:T(8,128)(2,1)}) %all-gather.5.cloned.1.call-update) | async-done | bytes 2097168 | tf_op jit(solution)/shard_map/all_gather | solution.py:128
  125.8 2.0 convolution_convert_fusion.1
  127.9 2.7 fusion.17
  130.6 2.3 copy.47
  132.9 2.7 fusion.14
  135.6 2.4 copy.50
  137.9 2.3 broadcast_add_fusion.1
  142.4 147.3 %all-reduce = f32[2048]{0:T(1024)S(1)} all-reduce(f32[2048]{0:T(1024)S(1)} %dynamic-update-slice), channel_id=2, replica_groups=mesh['dp'=2,'ctx'=64,'head'=2] {'ctx'}, use_global_device_ids=true, to_apply=%add | all-reduce | flops 2048 | bytes 16384
  292.0 227.4 %all-gather.9.cloned.1.call-done = f32[64,64,2048]{2,1,0:T(8,128)} async-done(((f32[1,64,2048]{2,1,0:T(8,128)}), f32[64,64,2048]{2,1,0:T(8,128)}) %all-gather.9.cloned.1.call-update) | async-done | bytes 33554448 | tf_op jit(solution)/shard_map/all_gather | solution.py:15
  519.5 1.3 copy.64
  520.9 3.1 convolution_bitcast_fusion.2
  523.9 370.8 %all-gather.7.cloned.1.call-done = f32[64,64,2048]{2,1,0:T(8,128)} async-done(((f32[1,64,2048]{2,1,0:T(8,128)}), f32[64,64,2048]{2,1,0:T(8,128)}) %all-gather.7.cloned.1.call-update) | async-done | bytes 33554448 | tf_op jit(solution)/shard_map/all_gather | solution.py:15
  894.8 90.5 %while.26 = (s32[]{:T(128)}, f32[64,2048]{1,0:T(8,128)S(1)}, s32[]{:T(128)}, f32[64,32]{1,0:T(8,128)S(1)}, f32[64,64,2048]{2,1,0:T(8,128)}, /*index=5*/s32[]{:T(128)}, s32[]{:T(128)}, s32[]{:T(128)}, s32[]{:T(128)}) while((s32[]{:T(128)}, f32[64,2048]{1,0:T(8,128)S(1)}, s32[]{:T(128)}, f32[64,32]{1,0:T(8,128)S(1)}, f32[64,64,2048]{2,1,0:T(8,128)}, ...), condition=%wide.region_3.4_spmd, body=%wide.region_2.3_spmd.sunk | while | flops 262150 | bytes 1606171 | solution.py:24
  896.4 1.3 bitcast_add_fusion.4
  897.8 1.3 bitcast_add_fusion.4
  899.3 1.3 bitcast_add_fusion.4
  900.7 1.3 bitcast_add_fusion.4
  902.2 1.3 bitcast_add_fusion.4
  903.6 1.3 bitcast_add_fusion.4
  905.0 1.3 bitcast_add_fusion.4
  906.5 1.3 bitcast_add_fusion.4
  909.3 1.3 bitcast_add_fusion.4
  910.8 1.3 bitcast_add_fusion.4
  912.2 1.3 bitcast_add_fusion.4
  913.7 1.3 bitcast_add_fusion.4
  915.1 1.3 bitcast_add_fusion.4
  916.5 1.3 bitcast_add_fusion.4
  918.0 1.3 bitcast_add_fusion.4
  919.4 1.3 bitcast_add_fusion.4
  920.8 1.3 bitcast_add_fusion.4
  923.7 1.3 bitcast_add_fusion.4
  925.1 1.3 bitcast_add_fusion.4
  926.6 1.3 bitcast_add_fusion.4
  928.0 1.3 bitcast_add_fusion.4
  929.5 1.3 bitcast_add_fusion.4
  930.9 1.3 bitcast_add_fusion.4
  932.3 1.3 bitcast_add_fusion.4
  933.8 1.3 bitcast_add_fusion.4
  936.6 1.3 bitcast_add_fusion.4
  938.1 1.3 bitcast_add_fusion.4
  939.5 1.3 bitcast_add_fusion.4
  941.0 1.3 bitcast_add_fusion.4
  942.4 1.3 bitcast_add_fusion.4
  943.8 1.3 bitcast_add_fusion.4
  945.3 1.3 bitcast_add_fusion.4
  946.7 1.3 bitcast_add_fusion.4
  948.1 1.3 bitcast_add_fusion.4
  951.0 1.3 bitcast_add_fusion.4
  952.4 1.3 bitcast_add_fusion.4
  953.9 1.3 bitcast_add_fusion.4
  955.3 1.3 bitcast_add_fusion.4
  956.8 1.3 bitcast_add_fusion.4
  958.2 1.3 bitcast_add_fusion.4
  985.3 1.4 copy.63
  986.7 3.1 convolution_bitcast_fusion.3
  990.1 2.7 fusion
  992.8 5.6 copy.61
  998.7 3.5 convolution_convert_fusion
  1005.8 2.0 copy.54
  1011.3 590.0 %reduce-scatter.7.cloned.1.call-done = f32[32,256]{1,0:T(8,128)} async-done(((f32[4096,256]{1,0:T(8,128)}), f32[32,256]{1,0:T(8,128)}) %reduce-scatter.7.cloned.1.call-update) | async-done | bytes 32784
  1602.9 114.7 %reduce-scatter.5.cloned.1.call-done = bf16[128,2048]{1,0:T(8,128)(2,1)} async-done(((bf16[128,4096]{1,0:T(8,128)(2,1)}), bf16[128,2048]{1,0:T(8,128)(2,1)}) %reduce-scatter.5.cloned.1.call-update) | async-done | bytes 524304 | tf_op jit(solution)/shard_map/reduce_scatter | solution.py:201
  (291 shorter events, 55.7 us)
Async XLA Ops:
  7.2 118.6 %copy-start = (bf16[1,128,4096]{2,1,0:T(8,128)(2,1)S(1)}, bf16[1,128,4096]{2,1,0:T(8,128)(2,1)}, u32[]{:S(2)}) copy-start(bf16[1,128,4096]{2,1,0:T(8,128)(2,1)} %param.11) | copy-start | bytes 3145732
  7.2 3.0 copy-start.13
  7.2 118.6 %all-gather.5.cloned.1.call-start = ((), (), s32[]{:S(2)}) async-start(), calls=%async_computation.2 | async-start | bytes 2113536 | tf_op jit(solution)/shard_map/all_gather | solution.py:128
  8.7 510.7 %all-gather.9.cloned.1.call-start = ((), (), s32[]{:S(2)}) async-start(), calls=%async_computation.4 | async-start | bytes 34078720 | tf_op jit(solution)/shard_map/all_gather | solution.py:15
  10.1 2.2 copy-start.14
  12.3 277.5 %copy-start.2 = (f32[1,128,2048]{1,2,0:T(8,128)}, f32[1,128,2048]{1,2,0:T(8,128)S(1)}, u32[]{:S(2)}) copy-start(f32[1,128,2048]{1,2,0:T(8,128)S(1)} %convert_element_type.117) | copy-start | bytes 3145732
  135.6 5.4 copy-start.16
  140.2 754.5 %all-gather.7.cloned.1.call-start = ((), (), s32[]{:S(2)}) async-start(), calls=%async_computation.3 | async-start | bytes 34078720 | tf_op jit(solution)/shard_map/all_gather | solution.py:15
  141.0 1460.4 %reduce-scatter.7.cloned.1.call-start = ((), (), s32[]{:S(2)}) async-start(), calls=%async_computation.6 | async-start | bytes 4227072
  289.8 1.1 copy-start.7
  290.1 0.8 copy-start.11
  519.5 1.4 copy-start.6
  894.8 92.0 %copy-start.8 = (bf16[1,128,2048]{1,2,0:T(8,128)(2,1)S(1)}, bf16[1,128,2048]{1,2,0:T(8,128)(2,1)}, u32[]{:S(2)}) copy-start(bf16[1,128,2048]{1,2,0:T(8,128)(2,1)} %copy.46) | copy-start | bytes 1572868
  998.5 4.7 copy-start.5
  998.5 719.1 %reduce-scatter.5.cloned.1.call-start = ((), (), s32[]{:S(2)}) async-start(), calls=%async_computation.5 | async-start | bytes 1572864 | tf_op jit(solution)/shard_map/reduce_scatter | solution.py:201
  1003.2 1.0 copy-start.9
  1003.2 1.4 copy-start.12
  1003.2 1.4 copy-start.15
  1004.6 3.3 copy-start.4
  1007.8 1.2 copy-start.3
  1007.8 1.5 copy-start.10
  1009.4 708.2 %copy-start.1 = (bf16[1,128,4096]{2,1,0:T(8,128)(2,1)S(1)}, bf16[1,128,4096]{2,1,0:T(8,128)(2,1)}, u32[]{:S(2)}) copy-start(bf16[1,128,4096]{2,1,0:T(8,128)(2,1)} %param.11) | copy-start | bytes 3145732
Sparse Core Ops, SparseCore 0:
  12.2 113.5 all-gather.4
  140.3 379.0 all-gather.8
  521.8 372.8 all-gather.6
  998.6 602.7 reduce-scatter.6
  1604.3 113.2 reduce-scatter.4
where the time goes:
time: 1730 us; the launch traced here: 1720 us
  waiting for transfers between devices  1410 us (82%)
  blocking collectives  147 us (8%)
  other arithmetic  85.1 us (5%)
  local copies, waits for them, and re-layouts  36.8 us (2%)
  matrix products  24.6 us (1%)
    all_gather x2, waiting for transfers between devices, carried_in(): gathered = jax.tree.map(lambda a: lax.all_gather(a, axis), part)  598 us
    unnamed x6, waiting for transfers between devices  591 us
    unnamed x1, blocking collectives  147 us
    reduce_scatter x1, waiting for transfers between devices, body(): lax.psum_scatter(input_terms.astype(jnp.bfloat16), 'head', scatter_dimens...  115 us
    all_gather x1, waiting for transfers between devices, body(): lax.all_gather(weight_local, ('dp', 'ctx'), axis=0, tiled=True)  110 us
    add x63, other arithmetic, chain(): earlier[1] * jnp.repeat(later[0], HEAD_DIM)[None, :] + later[1]  78.9 us
  transfers between devices with their start and end apart: 5, of which 5 were waited for; matrix products, arithmetic and copies ran while one was open for 2% of the time, Pallas kernels for 0%

commit v1 on v0

--- a/solution.py
+++ b/solution.py
@@ -125,7 +125,8 @@
     tok_rows = tokens.shape[0]
     weight_local = proj_weight.reshape(proj_weight.shape[0], -1)
     col_count = weight_local.shape[1]
-    weight_full = lax.all_gather(weight_local, ("dp", "ctx"), axis=0, tiled=True)
+    stack = jnp.stack([weight_local] * lax.axis_size(("dp", "ctx")))
+    weight_full = jnp.concatenate(lax.all_to_all(stack, ("dp", "ctx"), 0, 0), axis=0)
     bc_sums = jnp.dot(tokens, weight_full, preferred_element_type=jnp.float32)
     group_count = col_count // (2 * STATE)
     head_count = values_in.shape[2] // HEAD_DIM

time: 1730 us -> 1670 us (0.965)
  waiting for transfers between devices: 1410 us -> 1340 us
    all_gather x1 -> x0, waiting for transfers between devices: 110 us -> none  [body(): lax.all_gather(weight_local, ('dp', 'ctx'), axis=0, tiled=True)]
    unnamed x6 -> x5, waiting for transfers between devices: 591 us -> 685 us
    all_gather x2, waiting for transfers between devices: 598 us -> 504 us  [carried_in(): gathered = jax.tree.map(lambda a: lax.all_gather(a, axis), part)]
    all_to_all x0 -> x1, waiting for transfers between devices: none -> 39.1 us  [body(): lax.all_to_all(stack, ('dp', 'ctx'), 0, 0)]
  transfers between devices with their start and end apart: 5 -> 5, of which waited for: 5 -> 5; matrix products, arithmetic and copies ran while one was open for 2% -> 7% of each run, Pallas kernels for 0% -> 0%
where the time goes in v1:
time: 1670 us; the launch traced here: 1660 us
  waiting for transfers between devices  1340 us (80%)
  blocking collectives  144 us (9%)
  other arithmetic  91.3 us (5%)
  local copies, waits for them, and re-layouts  35.6 us (2%)
  matrix products  20.4 us (1%)
    unnamed x5, waiting for transfers between devices  685 us
    all_gather x2, waiting for transfers between devices, carried_in(): gathered = jax.tree.map(lambda a: lax.all_gather(a, axis), part)  504 us
    unnamed x1, blocking collectives  144 us
    reduce_scatter x1, waiting for transfers between devices, body(): lax.psum_scatter(input_terms.astype(jnp.bfloat16), 'head', scatter_dimens...  110 us
    add x63, other arithmetic, chain(): earlier[1] * jnp.repeat(later[0], HEAD_DIM)[None, :] + later[1]  79.2 us
    all_to_all x1, waiting for transfers between devices, body(): lax.all_to_all(stack, ('dp', 'ctx'), 0, 0)  39.1 us
  transfers between devices with their start and end apart: 5, of which 5 were waited for; matrix products, arithmetic and copies ran while one was open for 7% of the time, Pallas kernels for 0%

profile of v1, /device:TPU:1, one launch (start us, length us, event | category | flops | bytes accessed | tf_op | source)
XLA Modules:
  0.0 1663.2 jit_solution(827760737881968302)
XLA Ops:
  8.0 1.6 stack.15
  9.6 16.3 all-to-all-start
  26.0 2.0 copy.44
  28.0 2.1 convert_element_type.116
  30.1 2.0 copy.45
  32.2 2.1 convert_element_type.117
  34.9 2.0 copy.46
  37.0 2.6 multiply_convert_fusion
  39.7 39.1 %all-to-all-done = bf16[128,32,256]{2,1,0:T(8,128)(2,1)S(1)} async-done(((bf16[128,32,256]{2,1,0:T(8,128)(2,1)}), bf16[128,32,256]{2,1,0:T(8,128)(2,1)S(1)}, u32[]{:S(2)}, u32[]{:S(2)}) %all-to-all-start) | async-done | bytes 2097184 | tf_op jit(solution)/shard_map/all_to_all | solution.py:129
  79.3 2.8 fusion.19
  82.1 1.5 copy.47
  83.6 1.7 fusion.16
  89.0 144.2 %all-reduce = f32[2048]{0:T(1024)S(1)} all-reduce(f32[2048]{0:T(1024)S(1)} %dynamic-update-slice), channel_id=2, replica_groups=mesh['dp'=2,'ctx'=64,'head'=2] {'ctx'}, use_global_device_ids=true, to_apply=%add | all-reduce | flops 2048 | bytes 16384
  233.2 225.4 %all-gather.4.cloned.1.call-done = f32[64,64,2048]{2,1,0:T(8,128)} async-done(((f32[1,64,2048]{2,1,0:T(8,128)}), f32[64,64,2048]{2,1,0:T(8,128)}) %all-gather.4.cloned.1.call-update) | async-done | bytes 33554448 | tf_op jit(solution)/shard_map/all_gather | solution.py:15
  458.6 90.8 %while.26 = (s32[]{:T(128)}, f32[64,2048]{1,0:T(8,128)S(1)}, s32[]{:T(128)}, f32[64,32]{1,0:T(8,128)S(1)}, f32[64,64,2048]{2,1,0:T(8,128)}, /*index=5*/s32[]{:T(128)}, s32[]{:T(128)}, s32[]{:T(128)}, s32[]{:T(128)}) while((s32[]{:T(128)}, f32[64,2048]{1,0:T(8,128)S(1)}, s32[]{:T(128)}, f32[64,32]{1,0:T(8,128)S(1)}, f32[64,64,2048]{2,1,0:T(8,128)}, ...), condition=%wide.region_3.4_spmd, body=%wide.region_2.3_spmd.sunk | while | flops 262150 | bytes 1606171 | solution.py:24
  458.8 1.3 bitcast_add_fusion.4
  460.3 1.3 bitcast_add_fusion.4
  461.7 1.3 bitcast_add_fusion.4
  463.1 1.3 bitcast_add_fusion.4
  466.0 1.3 bitcast_add_fusion.4
  467.4 1.3 bitcast_add_fusion.4
  468.9 1.3 bitcast_add_fusion.4
  470.3 1.3 bitcast_add_fusion.4
  473.2 1.3 bitcast_add_fusion.4
  490.4 1.3 bitcast_add_fusion.4
  491.9 1.3 bitcast_add_fusion.4
  493.3 1.3 bitcast_add_fusion.4
  494.8 1.3 bitcast_add_fusion.4
  496.2 1.3 bitcast_add_fusion.4
  497.7 1.3 bitcast_add_fusion.4
  499.1 1.3 bitcast_add_fusion.4
  500.6 1.3 bitcast_add_fusion.4
  502.0 1.3 bitcast_add_fusion.4
  503.5 1.3 bitcast_add_fusion.4
  504.9 1.3 bitcast_add_fusion.4
  506.4 1.3 bitcast_add_fusion.4
  520.7 1.3 bitcast_add_fusion.4
  522.2 1.3 bitcast_add_fusion.4
  523.6 1.3 bitcast_add_fusion.4
  525.1 1.3 bitcast_add_fusion.4
  526.5 1.3 bitcast_add_fusion.4
  527.9 1.3 bitcast_add_fusion.4
  529.4 1.3 bitcast_add_fusion.4
  530.8 1.3 bitcast_add_fusion.4
  532.3 1.3 bitcast_add_fusion.4
  533.7 1.3 bitcast_add_fusion.4
  535.2 1.3 bitcast_add_fusion.4
  536.6 1.3 bitcast_add_fusion.4
  538.1 1.3 bitcast_add_fusion.4
  539.5 1.3 bitcast_add_fusion.4
  541.0 1.3 bitcast_add_fusion.4
  549.8 1.9 convolution_bitcast_fusion.3
  551.6 1.6 fusion.27
  553.2 278.8 %all-gather.6.cloned.1.call-done = f32[64,64,2048]{2,1,0:T(8,128)} async-done(((f32[1,64,2048]{2,1,0:T(8,128)}), f32[64,64,2048]{2,1,0:T(8,128)}) %all-gather.6.cloned.1.call-update) | async-done | bytes 33554448 | tf_op jit(solution)/shard_map/all_gather | solution.py:15
  833.1 1.9 convolution_bitcast_fusion.2
  835.0 3.0 bitcast_multiply_fusion.2
  839.4 2.7 fusion
  842.1 5.6 copy.61
  847.8 1.5 copy-done.2
  849.3 1.8 convolution_convert_fusion
  852.4 2.5 fusion.11
  854.9 2.0 copy.54
  860.5 684.5 %reduce-scatter.7.cloned.1.call-done = f32[32,256]{1,0:T(8,128)} async-done(((f32[4096,256]{1,0:T(8,128)}), f32[32,256]{1,0:T(8,128)}) %reduce-scatter.7.cloned.1.call-update) | async-done | bytes 32784
  1546.6 110.1 %reduce-scatter.5.cloned.1.call-done = bf16[128,2048]{1,0:T(8,128)(2,1)} async-done(((bf16[128,4096]{1,0:T(8,128)(2,1)}), bf16[128,2048]{1,0:T(8,128)(2,1)}) %reduce-scatter.5.cloned.1.call-update) | async-done | bytes 524304 | tf_op jit(solution)/shard_map/reduce_scatter | solution.py:202
  (290 shorter events, 57.9 us)
Async XLA Ops:
  7.2 71.5 %copy-start = (bf16[1,128,4096]{2,1,0:T(8,128)(2,1)S(1)}, bf16[1,128,4096]{2,1,0:T(8,128)(2,1)}, u32[]{:S(2)}) copy-start(bf16[1,128,4096]{2,1,0:T(8,128)(2,1)} %param.11) | copy-start | bytes 3145732
  9.6 69.1 %all-to-all-start = ((bf16[128,32,256]{2,1,0:T(8,128)(2,1)}), bf16[128,32,256]{2,1,0:T(8,128)(2,1)S(1)}, u32[]{:S(2)}, u32[]{:S(2)}) async-start(bf16[128,32,256]{2,1,0:T(8,128)(2,1)} %stack.15), calls=%async_computation | async-start | bytes 4194304 | tf_op jit(solution)/shard_map/all_to_all | solution.py:129
  25.9 432.7 %all-gather.4.cloned.1.call-start = ((), (), s32[]{:S(2)}) async-start(), calls=%async_computation.3 | async-start | bytes 34078720 | tf_op jit(solution)/shard_map/all_gather | solution.py:15
  28.0 6.3 copy-start.14
  78.7 3.4 copy-start.1
  85.3 2.2 copy-start.16
  86.8 745.3 %all-gather.6.cloned.1.call-start = ((), (), s32[]{:S(2)}) async-start(), calls=%async_computation.4 | async-start | bytes 34078720 | tf_op jit(solution)/shard_map/all_gather | solution.py:15
  87.5 1457.5 %reduce-scatter.7.cloned.1.call-start = ((), (), s32[]{:S(2)}) async-start(), calls=%async_computation.6 | async-start | bytes 4227072
  458.6 91.1 %copy-start.9 = (bf16[1,128,2048]{1,2,0:T(8,128)(2,1)S(1)}, bf16[1,128,2048]{1,2,0:T(8,128)(2,1)}, u32[]{:S(2)}) copy-start(bf16[1,128,2048]{1,2,0:T(8,128)(2,1)} %copy.46) | copy-start | bytes 1572868
  832.1 1.0 copy-start.8
  832.6 5.3 copy-start.3
  832.6 2.4 copy-start.5
  835.0 3.0 copy-start.10
  838.0 1.1 copy-start.13
  847.7 1.6 copy-start.2
  847.8 4.4 copy-start.15
  847.8 808.9 %reduce-scatter.5.cloned.1.call-start = ((), (), s32[]{:S(2)}) async-start(), calls=%async_computation.5 | async-start | bytes 1572864 | tf_op jit(solution)/shard_map/reduce_scatter | solution.py:202
  851.2 1.2 copy-start.12
  852.4 4.6 copy-start.4
  857.0 1.2 copy-start.6
  857.0 1.5 copy-start.7
  857.0 1.7 copy-start.11
Sparse Core Ops, SparseCore 0:
  86.9 371.6 all-gather.3
  460.4 371.6 all-gather.5
  847.9 697.0 reduce-scatter.6
  1547.9 108.7 reduce-scatter.4
